TPU v7x, 32 devices: a whole 2x2x4 slice. The times are simulated.
32 devices in a mesh: space: 4 (over z), dp: 8 (over y, x, core).
Axes of the slice: x: 2, y: 2, z: 4, core: 2. Of those that a mesh axis runs over, the one named last changes fastest.
Arguments:
- features: bfloat16 [8, 12, 128, 320], P('dp', 'space'), may hold values from -6 to 6
- cotangent: bfloat16 [8, 12, 128, 320], P('dp', 'space'), may hold values from -6 to 6
- norm_gain: float32 [320], replicated, may hold values from 0.1 to 1.9
- norm_bias: float32 [320], replicated, may hold values from -0.5 to 0.5
- weight: bfloat16 [2880, 320], P('dp'), may hold values from -0.109375 to 0.109375
- moment_one: float32 [2880, 320], P('dp'), may hold values from -332.55374 to 332.55374
- moment_two: float32 [2880, 320], P('dp'), may hold values from 768 to 6144
- heights: int32 [8], P('dp'), may hold values from 6 to 12, as said below
- widths: int32 [8], P('dp'), may hold values from 64 to 128, as said below
Outputs:
- block_out: bfloat16 [8, 12, 128, 320], P('dp', 'space')
- input_grad: bfloat16 [8, 12, 128, 320], P('dp', 'space')
- weight_grad: float32 [2880, 320], P('dp')
- adam_update: float32 [2880, 320], P('dp')
Inputs may be any that keep to these rules, and one draw needn't show every extreme that they name: Image i occupies canvas rows 0 to heights[i] - 1; some image has all 12 rows. Image i occupies canvas columns 0 to widths[i] - 1; some image has all 128 columns.
All inputs are finite; a program needn't handle non-finite values.
Results may differ from a plain program's by a relative error of at most 0.017.
Values may be sent and summed in bfloat16 or wider, within the bound.
No kernel may reach another device: no remote copies, remote signals or barrier semaphores. Data moves between devices by JAX's collectives and lax.ppermute only.
A program may use at most 64 MiB of HBM per device.

v0:
```python
import jax
import jax.numpy as jnp
from jax import lax
from jax.sharding import PartitionSpec as P

GROUPS = 32


def with_halo(cells, sides, width):
    for axis, dim in sides:
        count = lax.axis_size(axis)
        ends = count - 1
        head = lax.slice_in_dim(cells, 0, width, axis=dim)
        tail = lax.slice_in_dim(cells, cells.shape[dim] - width, cells.shape[dim], axis=dim)
        cells = jnp.concatenate(
            [
                lax.ppermute(tail, axis, [(i, (i + 1) % count) for i in range(ends)]),
                cells,
                lax.ppermute(head, axis, [((i + 1) % count, i) for i in range(ends)]),
            ],
            axis=dim,
        )
    return cells


def space_sum(parts, axis):
    count = lax.axis_size(axis)
    if count & count - 1:
        return lax.psum(parts, axis)
    step = 1
    while step < count:
        pairs = [(i, i ^ step) for i in range(count)]
        parts = tuple((p + q for p, q in zip(parts, lax.ppermute(parts, axis, pairs))))
        step *= 2
    return parts


def group_sum(values, groups):
    height_dev, width_dev, channels = values.shape
    return values.reshape(height_dev, width_dev, groups, channels // groups).sum(axis=(0, 1, 3))


def spread_groups(statistic, channels):
    return jnp.repeat(statistic, channels // statistic.shape[0])


def pad_columns(padded_rows):
    return jnp.pad(padded_rows, ((0, 0), (1, 1), (0, 0)))


def local(
    features, cotangent, norm_gain, norm_bias, weight, moment_one, moment_two, heights, widths
):
    latent = features[0]
    height_dev, width_dev, channels = latent.shape
    row_ids = lax.axis_index("space") * height_dev + jnp.arange(height_dev, dtype=jnp.int32)
    inside = (
        (row_ids < heights[0])[:, None]
        & (jnp.arange(width_dev, dtype=jnp.int32) < widths[0])[None, :]
    ).astype(jnp.float32)[..., None]
    cell_count = (heights[0] * widths[0] * (channels // GROUPS)).astype(jnp.float32)
    gathered = lax.all_gather(weight, "dp", axis=0, tiled=True)
    tap_weights = gathered.reshape(9, channels, channels)
    values = latent.astype(jnp.float32) * inside
    group_total, squares = space_sum(
        (group_sum(values, GROUPS), group_sum(values * values, GROUPS)), "space"
    )
    center = group_total / cell_count
    spread = squares / cell_count - center * center
    inverse = lax.rsqrt(spread + 1e-05)
    normed = (values - spread_groups(center, channels)) * spread_groups(inverse, channels) * inside
    before = normed * norm_gain + norm_bias
    activated = (jax.nn.silu(before) * inside).astype(jnp.bfloat16)
    act_pad = pad_columns(with_halo(activated, (("space", 0),), 1))
    output = jnp.zeros((height_dev * width_dev, channels), jnp.float32)
    for row_off in range(3):
        for col_off in range(3):
            window = act_pad[row_off : row_off + height_dev, col_off : col_off + width_dev].reshape(
                -1, channels
            )
            output = output + jnp.dot(
                window, tap_weights[row_off * 3 + col_off], preferred_element_type=jnp.float32
            )
    block_out = (output.reshape(height_dev, width_dev, channels) * inside).astype(jnp.bfloat16)
    masked = cotangent[0] * inside.astype(jnp.bfloat16)
    cot_pad = pad_columns(with_halo(masked, (("space", 0),), 1))
    flat_cot = masked.reshape(-1, channels)
    upstream = jnp.zeros((height_dev * width_dev, channels), jnp.float32)
    tap_grads = []
    for row_off in range(3):
        for col_off in range(3):
            tap_index = row_off * 3 + col_off
            window = act_pad[row_off : row_off + height_dev, col_off : col_off + width_dev].reshape(
                -1, channels
            )
            tap_grads.append(
                lax.dot_general(
                    window, flat_cot, (((0,), (0,)), ((), ())), preferred_element_type=jnp.float32
                )
            )
            cot_window = cot_pad[
                2 - row_off : 2 - row_off + height_dev, 2 - col_off : 2 - col_off + width_dev
            ].reshape(-1, channels)
            upstream = upstream + lax.dot_general(
                cot_window,
                tap_weights[tap_index],
                (((1,), (1,)), ((), ())),
                preferred_element_type=jnp.float32,
            )
    weight_terms = jnp.stack(tap_grads).reshape(9 * channels, channels)
    gate_sig = jax.nn.sigmoid(before)
    silu_slope = gate_sig * (1.0 + before * (1.0 - gate_sig))
    scaled = upstream.reshape(height_dev, width_dev, channels) * silu_slope * inside * norm_gain
    local_first = group_sum(scaled, GROUPS)
    local_second = group_sum(scaled * normed, GROUPS)
    dp_size = lax.axis_size("dp")
    grad_piece = lax.psum_scatter(
        weight_terms.astype(jnp.bfloat16).reshape(dp_size, -1, channels),
        "dp",
        scatter_dimension=0,
        tiled=False,
    )
    sum_first, sum_second = space_sum((local_first, local_second), "space")
    grad_piece = lax.psum(grad_piece, "space").astype(jnp.float32)
    first = sum_first / cell_count
    second = sum_second / cell_count
    input_grad = (
        spread_groups(inverse, channels)
        * (scaled - spread_groups(first, channels) - normed * spread_groups(second, channels))
        * inside
    ).astype(jnp.bfloat16)
    first_new = 0.9 * moment_one + 0.1 * grad_piece
    second_new = 0.999 * moment_two + 0.001 * grad_piece * grad_piece
    adam_update = first_new / (1.0 - 0.9**10) / (jnp.sqrt(second_new / (1.0 - 0.999**10)) + 1e-08)
    return (block_out[None], input_grad[None], grad_piece, adam_update)


def solution(mesh):
    placed = (
        P("dp", "space", None, None),
        P("dp", "space", None, None),
        P(),
        P(),
        P("dp", None),
        P("dp", None),
        P("dp", None),
        P("dp"),
        P("dp"),
    )
    return jax.shard_map(
        local,
        mesh=mesh,
        in_specs=placed,
        out_specs=(
            P("dp", "space", None, None),
            P("dp", "space", None, None),
            P("dp", None),
            P("dp", None),
        ),
        check_vma=False,
    )
```

profile of v0, /device:TPU:0, one launch (start us, length us, event | category | flops | bytes accessed | tf_op | source)
XLA Modules:
  0.0 191.6 jit_solution(13779045567825138440)
XLA Ops:
  8.6 1.1 multiply_reduce_fusion.1
  10.0 3.1 %collective-permute-start = (f32[32]{0:T(128)S(1)}, f32[32]{0:T(128)S(1)}, u32[]{:S(2)}, u32[]{:S(2)}) collective-permute-start(f32[32]{0:T(128)S(1)} %reduce_sum.51), channel_id=1, source_target_pairs={{0,8},{8,0},{16,24},{24,16},{1,9},{9,1},{17,25},{25,17},{2,10},{10... | collective-permute-start | bytes 392 | tf_op jit(solution)/shard_map/ppermute | solution.py:33
  13.4 1.2 collective-permute-done
  14.6 3.0 %collective-permute-start.1 = (f32[32]{0:T(128)S(1)}, f32[32]{0:T(128)S(1)}, u32[]{:S(2)}, u32[]{:S(2)}) collective-permute-start(f32[32]{0:T(128)S(1)} %add.163), channel_id=1, source_target_pairs={{0,16},{8,24},{16,0},{24,8},{1,17},{9,25},{17,1},{25,9},{2,18},{10... | collective-permute-start | bytes 392 | tf_op jit(solution)/shard_map/ppermute | solution.py:33
  17.6 1.9 collective-permute-start.3
  19.5 2.6 %collective-permute-done.3 = f32[32]{0:T(128)S(1)} collective-permute-done((f32[32]{0:T(128)S(1)}, f32[32]{0:T(128)S(1)}, u32[]{:S(2)}, u32[]{:S(2)}) %collective-permute-start.3) | collective-permute-done | bytes 160 | tf_op jit(solution)/shard_map/ppermute | solution.py:33
  22.5 1.3 multiply_convert_fusion.4
  23.7 3.5 %collective-permute-start.4 = (bf16[1,128,320]{1,2,0:T(8,128)(2,1)S(1)}, bf16[1,128,320]{1,2,0:T(8,128)(2,1)S(1)}, u32[]{:S(2)}, u32[]{:S(2)}) collective-permute-start(bf16[1,128,320]{1,2,0:T(8,128)(2,1)S(1)} %get-tuple-element.30), channel_id=1, source_target_pairs={{0,8},{8,16},{16,24},{1,9},{9,17},{17,25},{2,10},{10,18},{18,26},{... | collective-permute-start | bytes 245768 | tf_op jit(solution)/shard_map/ppermute | solution.py:17
  27.2 1.3 collective-permute-start.5
  28.5 1.0 bitcast_multiply_fusion.2
  29.5 4.1 %collective-permute-done.5 = bf16[1,128,320]{1,2,0:T(8,128)(2,1)S(1)} collective-permute-done((bf16[1,128,320]{1,2,0:T(8,128)(2,1)S(1)}, bf16[1,128,320]{1,2,0:T(8,128)(2,1)S(1)}, u32[]{:S(2)}, u32[]{:S(2)}) %collective-permute-start.5) | collective-permute-done | bytes 81952 | tf_op jit(solution)/shard_map/ppermute | solution.py:19
  34.0 1.0 fusion.29
  35.0 1.0 fusion.15
  36.0 1.1 fusion.27
  37.1 1.0 fusion.25
  38.1 1.2 fusion.23
  39.4 1.1 fusion.21
  40.4 1.0 fusion.19
  41.4 1.1 fusion.13
  42.5 1.1 fusion.17
  43.6 4.2 %copy.68 = bf16[8,360,320]{1,2,0:T(8,128)(2,1)} copy(bf16[8,360,320]{2,1,0:T(8,128)(2,1)} %bitcast.48) | data formatting | bytes 3686400 | tf_op jit(solution)/shard_map/convert_element_type | solution.py:118
  47.8 38.9 %reduce-scatter.2.cloned.1.call-done = bf16[1,360,320]{1,2,0:T(8,128)(2,1)} async-done(((bf16[8,360,320]{1,2,0:T(8,128)(2,1)}), bf16[1,360,320]{1,2,0:T(8,128)(2,1)}) %reduce-scatter.2.cloned.1.call-update) | async-done | bytes 230416 | tf_op jit(solution)/shard_map/reduce_scatter | solution.py:117
  86.8 0.7 all-gather.3.cloned.1.call-update
  87.5 3.4 %collective-permute-start.6 = (bf16[1,128,320]{1,2,0:T(8,128)(2,1)S(1)}, bf16[1,128,320]{1,2,0:T(8,128)(2,1)S(1)}, u32[]{:S(2)}, u32[]{:S(2)}) collective-permute-start(bf16[1,128,320]{1,2,0:T(8,128)(2,1)S(1)} %get-tuple-element.26), channel_id=1, source_target_pairs={{0,8},{8,16},{16,24},{1,9},{9,17},{17,25},{2,10},{10,18},{18,26},{... | collective-permute-start | bytes 245768 | tf_op jit(solution)/shard_map/ppermute | solution.py:17
  90.9 1.3 collective-permute-start.7
  92.8 1.0 copy.49
  93.8 4.8 %collective-permute-done.7 = bf16[1,128,320]{1,2,0:T(8,128)(2,1)S(1)} collective-permute-done((bf16[1,128,320]{1,2,0:T(8,128)(2,1)S(1)}, bf16[1,128,320]{1,2,0:T(8,128)(2,1)S(1)}, u32[]{:S(2)}, u32[]{:S(2)}) %collective-permute-start.7) | collective-permute-done | bytes 81952 | tf_op jit(solution)/shard_map/ppermute | solution.py:19
  98.7 0.6 copy-done.15
  100.0 0.9 copy.56
  100.9 1.7 pad_maximum_fusion
  102.6 1.8 copy.57
  104.4 0.9 copy.58
  105.3 0.9 copy.59
  106.3 0.9 copy.61
  107.2 0.9 copy.62
  108.1 0.9 copy.63
  109.0 0.9 copy.64
  109.9 1.0 fusion.102
  110.9 1.2 copy.43
  112.1 0.9 copy.45
  113.0 0.9 copy.46
  113.9 0.9 copy.47
  114.8 0.9 copy.51
  115.7 0.9 copy.50
  117.1 7.1 %all-reduce.4.cloned.1.call-done = bf16[360,320]{0,1:T(8,128)(2,1)} async-done(((bf16[360,320]{0,1:T(8,128)(2,1)}), bf16[360,320]{0,1:T(8,128)(2,1)}) %all-reduce.4.cloned.1.call-update) | async-done | bytes 230416 | tf_op jit(solution)/shard_map/psum | solution.py:124
  124.2 2.3 %fusion.35 = (f32[360,320]{0,1:T(8,128)}, f32[360,320]{0,1:T(8,128)}) fusion(f32[360,320]{0,1:T(8,128)S(1)} %copy-done.11, f32[360,320]{0,1:T(8,128)} %param.14, bf16[360,320]{0,1:T(8,128)(2,1)} %all-reduce.4.cloned.1.call-done), kind=kLoop, calls=%fused_computation.65 | loop fusion | flops 1382400 | bytes 2073600 | tf_op jit(solution)/shard_map/div | solution.py:134
  126.5 27.0 %all-gather.3.cloned.1.call-done = bf16[8,360,320]{1,2,0:T(8,128)(2,1)} async-done(((bf16[1,360,320]{1,2,0:T(8,128)(2,1)}), bf16[8,360,320]{1,2,0:T(8,128)(2,1)}) %all-gather.3.cloned.1.call-update) | async-done | bytes 1843216 | tf_op jit(solution)/shard_map/all_gather | solution.py:62
  153.5 4.0 %copy.44 = bf16[8,360,320]{1,0,2:T(8,128)(2,1)} copy(bf16[8,360,320]{1,2,0:T(8,128)(2,1)} %all-gather.3.cloned.1.call-done) | data formatting | bytes 3686400 | tf_op jit(solution)/shard_map/all_gather | solution.py:62
  157.4 3.4 %reshape.284 = bf16[2880,320]{0,1:T(8,128)(2,1)S(1)} reshape(bf16[8,360,320]{1,0,2:T(8,128)(2,1)} %copy.44) | data formatting | bytes 3686400
  161.2 1.3 fusion.68
  164.3 0.5 fusion.2
  166.1 1.4 fusion.81
  167.5 1.5 convolution_add_fusion.8
  169.4 0.5 convolution_add_fusion.6
  170.4 0.5 convolution_add_fusion.4
  171.3 0.5 convolution_add_fusion.2
  172.0 0.7 fusion.100
  173.0 1.6 collective-permute-start.8
  174.7 0.6 collective-permute-start.10
  175.6 1.0 collective-permute-done.8
  176.6 2.4 %collective-permute-start.9 = (f32[32]{0:T(128)S(1)}, f32[32]{0:T(128)S(1)}, u32[]{:S(2)}, u32[]{:S(2)}) collective-permute-start(f32[32]{0:T(128)S(1)} %add.198), channel_id=1, source_target_pairs={{0,16},{8,24},{16,0},{24,8},{1,17},{9,25},{17,1},{25,9},{2,18},{10... | collective-permute-start | bytes 392 | tf_op jit(solution)/shard_map/ppermute | solution.py:33
  179.0 1.8 collective-permute-start.11
  181.0 2.4 %collective-permute-done.11 = f32[32]{0:T(128)S(1)} collective-permute-done((f32[32]{0:T(128)S(1)}, f32[32]{0:T(128)S(1)}, u32[]{:S(2)}, u32[]{:S(2)}) %collective-permute-start.11) | collective-permute-done | bytes 160 | tf_op jit(solution)/shard_map/ppermute | solution.py:33
  183.8 1.3 multiply_convert_fusion.1
  (100 shorter events, 9.2 us)
Async XLA Ops:
  7.2 79.6 %reduce-scatter.2.cloned.1.call-start = ((), (), s32[]{:S(2)}) async-start(), calls=%async_computation.1 | async-start | bytes 2211840 | tf_op jit(solution)/shard_map/reduce_scatter | solution.py:117
  10.0 4.6 %collective-permute-start = (f32[32]{0:T(128)S(1)}, f32[32]{0:T(128)S(1)}, u32[]{:S(2)}, u32[]{:S(2)}) collective-permute-start(f32[32]{0:T(128)S(1)} %reduce_sum.51), channel_id=1, source_target_pairs={{0,8},{8,0},{16,24},{24,16},{1,9},{9,1},{17,25},{25,17},{2,10},{10... | collective-permute-start | bytes 392 | tf_op jit(solution)/shard_map/ppermute | solution.py:33
  13.3 4.3 %collective-permute-start.2 = (f32[32]{0:T(128)S(1)}, f32[32]{0:T(128)S(1)}, u32[]{:S(2)}, u32[]{:S(2)}) collective-permute-start(f32[32]{0:T(128)S(1)} %reduce_sum.54), channel_id=1, source_target_pairs={{0,8},{8,0},{16,24},{24,16},{1,9},{9,1},{17,25},{25,17},{2,10},{10... | collective-permute-start | bytes 392 | tf_op jit(solution)/shard_map/ppermute | solution.py:33
  14.6 4.9 %collective-permute-start.1 = (f32[32]{0:T(128)S(1)}, f32[32]{0:T(128)S(1)}, u32[]{:S(2)}, u32[]{:S(2)}) collective-permute-start(f32[32]{0:T(128)S(1)} %add.163), channel_id=1, source_target_pairs={{0,16},{8,24},{16,0},{24,8},{1,17},{9,25},{17,1},{25,9},{2,18},{10... | collective-permute-start | bytes 392 | tf_op jit(solution)/shard_map/ppermute | solution.py:33
  17.6 4.4 %collective-permute-start.3 = (f32[32]{0:T(128)S(1)}, f32[32]{0:T(128)S(1)}, u32[]{:S(2)}, u32[]{:S(2)}) collective-permute-start(f32[32]{0:T(128)S(1)} %add.165), channel_id=1, source_target_pairs={{0,16},{8,24},{16,0},{24,8},{1,17},{9,25},{17,1},{25,9},{2,18},{10... | collective-permute-start | bytes 392 | tf_op jit(solution)/shard_map/ppermute | solution.py:33
  23.7 5.8 %collective-permute-start.4 = (bf16[1,128,320]{1,2,0:T(8,128)(2,1)S(1)}, bf16[1,128,320]{1,2,0:T(8,128)(2,1)S(1)}, u32[]{:S(2)}, u32[]{:S(2)}) collective-permute-start(bf16[1,128,320]{1,2,0:T(8,128)(2,1)S(1)} %get-tuple-element.30), channel_id=1, source_target_pairs={{0,8},{8,16},{16,24},{1,9},{9,17},{17,25},{2,10},{10,18},{18,26},{... | collective-permute-start | bytes 245768 | tf_op jit(solution)/shard_map/ppermute | solution.py:17
  27.2 6.3 %collective-permute-start.5 = (bf16[1,128,320]{1,2,0:T(8,128)(2,1)S(1)}, bf16[1,128,320]{1,2,0:T(8,128)(2,1)S(1)}, u32[]{:S(2)}, u32[]{:S(2)}) collective-permute-start(bf16[1,128,320]{1,2,0:T(8,128)(2,1)S(1)} %get-tuple-element.31), channel_id=1, source_target_pairs={{8,0},{16,8},{24,16},{9,1},{17,9},{25,17},{10,2},{18,10},{26,18},{... | collective-permute-start | bytes 245768 | tf_op jit(solution)/shard_map/ppermute | solution.py:19
  34.0 4.2 %copy-start = (bf16[1,3,128,320]{2,3,1,0:T(8,128)(2,1)S(1)}, bf16[1,3,128,320]{2,3,1,0:T(8,128)(2,1)}, u32[]{:S(2)}) copy-start(bf16[1,3,128,320]{2,3,1,0:T(8,128)(2,1)} %param.9) | copy-start | bytes 737284
  34.0 4.2 %copy-start.10 = (bf16[1,3,128,320]{2,3,1,0:T(8,128)(2,1)S(1)}, bf16[1,3,128,320]{2,3,1,0:T(8,128)(2,1)}, u32[]{:S(2)}) copy-start(bf16[1,3,128,320]{2,3,1,0:T(8,128)(2,1)} %param.10) | copy-start | bytes 737284
  34.0 4.1 %copy-start.17 = (f32[320]{0:T(512)S(1)}, f32[320]{0:T(512)}, u32[]{:S(2)}) copy-start(f32[320]{0:T(512)} %param.12) | copy-start | bytes 3844
  34.0 4.1 %copy-start.18 = (f32[320]{0:T(512)S(1)}, f32[320]{0:T(512)}, u32[]{:S(2)}) copy-start(f32[320]{0:T(512)} %param.11) | copy-start | bytes 3844
  47.8 76.4 %all-reduce.4.cloned.1.call-start = ((), (), s32[]{:S(2)}) async-start(), calls=%async_computation.2 | async-start | bytes 491520 | tf_op jit(solution)/shard_map/psum | solution.py:124
  86.8 66.7 %all-gather.3.cloned.1.call-start = ((), (), s32[]{:S(2)}) async-start(), calls=%async_computation.3 | async-start | bytes 2211840 | tf_op jit(solution)/shard_map/all_gather | solution.py:62
  87.5 6.3 %collective-permute-start.6 = (bf16[1,128,320]{1,2,0:T(8,128)(2,1)S(1)}, bf16[1,128,320]{1,2,0:T(8,128)(2,1)S(1)}, u32[]{:S(2)}, u32[]{:S(2)}) collective-permute-start(bf16[1,128,320]{1,2,0:T(8,128)(2,1)S(1)} %get-tuple-element.26), channel_id=1, source_target_pairs={{0,8},{8,16},{16,24},{1,9},{9,17},{17,25},{2,10},{10,18},{18,26},{... | collective-permute-start | bytes 245768 | tf_op jit(solution)/shard_map/ppermute | solution.py:17
  90.9 7.7 %collective-permute-start.7 = (bf16[1,128,320]{1,2,0:T(8,128)(2,1)S(1)}, bf16[1,128,320]{1,2,0:T(8,128)(2,1)S(1)}, u32[]{:S(2)}, u32[]{:S(2)}) collective-permute-start(bf16[1,128,320]{1,2,0:T(8,128)(2,1)S(1)} %get-tuple-element.27), channel_id=1, source_target_pairs={{8,0},{16,8},{24,16},{9,1},{17,9},{25,17},{10,2},{18,10},{26,18},{... | collective-permute-start | bytes 245768 | tf_op jit(solution)/shard_map/ppermute | solution.py:19
  93.8 4.8 %copy-start.14 = (bf16[1,128,320]{1,2,0:T(8,128)(2,1)}, bf16[1,128,320]{1,2,0:T(8,128)(2,1)S(1)}, u32[]{:S(2)}) copy-start(bf16[1,128,320]{1,2,0:T(8,128)(2,1)S(1)} %collective-permute-done.6) | copy-start | bytes 245764
  98.7 0.6 copy-start.15
  113.0 11.2 %copy-start.11 = (f32[360,320]{0,1:T(8,128)S(1)}, f32[360,320]{0,1:T(8,128)}, u32[]{:S(2)}) copy-start(f32[360,320]{0,1:T(8,128)} %param.15) | copy-start | bytes 1382404
  160.8 1.7 copy-start.9
  160.8 2.1 %copy-start.8 = (bf16[3,128,320]{2,1,0:T(8,128)(2,1)S(1)}, bf16[3,128,320]{2,1,0:T(8,128)(2,1)}, u32[]{:S(2)}) copy-start(bf16[3,128,320]{2,1,0:T(8,128)(2,1)} %copy.45) | copy-start | bytes 737284
  161.2 2.1 %copy-start.7 = (bf16[3,128,320]{2,1,0:T(8,128)(2,1)S(1)}, bf16[3,128,320]{2,1,0:T(8,128)(2,1)}, u32[]{:S(2)}) copy-start(bf16[3,128,320]{2,1,0:T(8,128)(2,1)} %copy.46) | copy-start | bytes 737284
  162.5 1.1 copy-start.6
  163.3 1.1 copy-start.12
  166.1 2.9 %copy-start.5 = (bf16[3,128,320]{2,1,0:T(8,128)(2,1)S(1)}, bf16[3,128,320]{2,1,0:T(8,128)(2,1)}, u32[]{:S(2)}) copy-start(bf16[3,128,320]{2,1,0:T(8,128)(2,1)} %copy.58) | copy-start | bytes 737284
  166.1 3.3 %copy-start.4 = (bf16[3,128,320]{2,1,0:T(8,128)(2,1)S(1)}, bf16[3,128,320]{2,1,0:T(8,128)(2,1)}, u32[]{:S(2)}) copy-start(bf16[3,128,320]{2,1,0:T(8,128)(2,1)} %copy.59) | copy-start | bytes 737284
  169.4 1.0 copy-start.3
  169.9 1.0 copy-start.1
  170.3 1.0 copy-start.2
  170.9 1.1 copy-start.13
  170.9 1.1 copy-start.16
  173.0 3.6 %collective-permute-start.8 = (f32[32]{0:T(128)S(1)}, f32[32]{0:T(128)S(1)}, u32[]{:S(2)}, u32[]{:S(2)}) collective-permute-start(f32[32]{0:T(128)S(1)} %reduce_sum.72), channel_id=1, source_target_pairs={{0,8},{8,0},{16,24},{24,16},{1,9},{9,1},{17,25},{25,17},{2,10},{10... | collective-permute-start | bytes 392 | tf_op jit(solution)/shard_map/ppermute | solution.py:33
  174.7 4.3 %collective-permute-start.10 = (f32[32]{0:T(128)S(1)}, f32[32]{0:T(128)S(1)}, u32[]{:S(2)}, u32[]{:S(2)}) collective-permute-start(f32[32]{0:T(128)S(1)} %reduce_sum.75), channel_id=1, source_target_pairs={{0,8},{8,0},{16,24},{24,16},{1,9},{9,1},{17,25},{25,17},{2,10},{10... | collective-permute-start | bytes 392 | tf_op jit(solution)/shard_map/ppermute | solution.py:33
  176.6 4.4 %collective-permute-start.9 = (f32[32]{0:T(128)S(1)}, f32[32]{0:T(128)S(1)}, u32[]{:S(2)}, u32[]{:S(2)}) collective-permute-start(f32[32]{0:T(128)S(1)} %add.198), channel_id=1, source_target_pairs={{0,16},{8,24},{16,0},{24,8},{1,17},{9,25},{17,1},{25,9},{2,18},{10... | collective-permute-start | bytes 392 | tf_op jit(solution)/shard_map/ppermute | solution.py:33
  179.0 4.4 %collective-permute-start.11 = (f32[32]{0:T(128)S(1)}, f32[32]{0:T(128)S(1)}, u32[]{:S(2)}, u32[]{:S(2)}) collective-permute-start(f32[32]{0:T(128)S(1)} %add.200), channel_id=1, source_target_pairs={{0,16},{8,24},{16,0},{24,8},{1,17},{9,25},{17,1},{25,9},{2,18},{10... | collective-permute-start | bytes 392 | tf_op jit(solution)/shard_map/ppermute | solution.py:33
Sparse Core Ops, SparseCore 0:
  47.9 38.8 reduce-scatter.1
  89.2 34.9 all-reduce.3
  126.1 27.3 all-gather.2
where the time goes:
time: 192 us
  waiting for transfers between devices  89.9 us (47%)
  local copies, waits for them, and re-layouts  31.8 us (17%)
  starting transfers between devices  24 us (12%)
  matrix products  20.2 us (11%)
  between operations  15.6 us (8%)
  other arithmetic  10.2 us (5%)
    reduce_scatter x1, waiting for transfers between devices, local(): lax.psum_scatter(weight_terms.astype(jnp.bfloat16).reshape(dp_size, -1, c...  38.9 us
    all_gather x1, waiting for transfers between devices, local(): gathered = lax.all_gather(weight, 'dp', axis=0, tiled=True)  27 us
    ppermute x8, starting transfers between devices, space_sum(): lax.ppermute(parts, axis, pairs)  14.4 us
    dot_general x9, matrix products, local(): lax.dot_general(window, flat_cot, (((0,), (0,)), ((), ())), preferred_ele...  9.52 us
    ppermute x2, waiting for transfers between devices, with_halo(): lax.ppermute(head, axis, [((i + 1) % count, i) for i in range(ends)])  8.87 us
    slice x9, local copies, waits for them, and re-layouts, local(): cot_pad[2 - row_off:2 - row_off + height_dev, 2 - col_off:2 - col_off + w...  8.5 us
    ppermute x8, waiting for transfers between devices, space_sum(): lax.ppermute(parts, axis, pairs)  7.28 us
    slice x9, local copies, waits for them, and re-layouts, local(): act_pad[row_off:row_off + height_dev, col_off:col_off + width_dev]  7.13 us
  transfers between devices with their start and end apart: 15, of which 9 were waited for; matrix products, arithmetic and copies ran while one was open for 12% of the time, Pallas kernels for 0%

commit v1 on v0

--- a/solution.py
+++ b/solution.py
@@ -59,7 +59,12 @@
         & (jnp.arange(width_dev, dtype=jnp.int32) < widths[0])[None, :]
     ).astype(jnp.float32)[..., None]
     cell_count = (heights[0] * widths[0] * (channels // GROUPS)).astype(jnp.float32)
-    gathered = lax.all_gather(weight, "dp", axis=0, tiled=True)
+    ring = [weight]
+    for hop in range(7):
+        ring.append(lax.ppermute(ring[-1], "dp", [(dev, (dev + 1) % 8) for dev in range(8)]))
+    gathered = jnp.roll(
+        jnp.concatenate(ring[::-1], axis=0), (lax.axis_index("dp") + 1) * ring[0].shape[0], axis=0
+    )
     tap_weights = gathered.reshape(9, channels, channels)
     values = latent.astype(jnp.float32) * inside
     group_total, squares = space_sum(

time: 192 us -> 181 us (0.943)
  waiting for transfers between devices: 89.9 us -> 73.8 us
  matrix products: 20.2 us -> 30.3 us
  local copies, waits for them, and re-layouts: 31.8 us -> 27.8 us
  starting transfers between devices: 24 us -> 21.9 us
    reduce_scatter x1, waiting for transfers between devices: 38.9 us -> 0.02 us  [local(): lax.psum_scatter(weight_terms.astype(jnp.bfloat16).reshape(dp_size, -1, c...]
    ppermute x0 -> x7, waiting for transfers between devices: none -> 31.4 us  [local(): lax.ppermute(ring[-1], 'dp', [(dev, (dev + 1) % 8) for dev in range(8)])]
    all_gather x1 -> x0, waiting for transfers between devices: 27 us -> none  [local(): gathered = lax.all_gather(weight, 'dp', axis=0, tiled=True)]
    psum x1, waiting for transfers between devices: 7.13 us -> 32.7 us  [local(): grad_piece = lax.psum(grad_piece, 'space').astype(jnp.float32)]
    ppermute x2, waiting for transfers between devices: 8.87 us -> 0.01 us  [with_halo(): lax.ppermute(head, axis, [((i + 1) % count, i) for i in range(ends)])]
    dot_general x9, matrix products: 4.33 us -> 12.6 us  [local(): jnp.dot(window, tap_weights[row_off * 3 + col_off], preferred_element_typ...]
    dot_general x9, matrix products: 6.32 us -> 14.4 us  [local(): lax.dot_general(cot_window, tap_weights[tap_index], (((1,), (1,)), ((), (...]
    concatenate x0 -> x1, local copies, waits for them, and re-layouts: none -> 7.64 us  [local(): jnp.roll(jnp.concatenate(ring[::-1], axis=0), (lax.axis_index('dp') + 1)...]
  transfers between devices with their start and end apart: 15 -> 21, of which waited for: 9 -> 13; matrix products, arithmetic and copies ran while one was open for 12% -> 35% of each run, Pallas kernels for 0% -> 0%
where the time goes in v1:
time: 181 us; the launch traced here: 179 us
  waiting for transfers between devices  73.8 us (41%)
  matrix products  30.3 us (17%)
  local copies, waits for them, and re-layouts  27.8 us (15%)
  starting transfers between devices  21.9 us (12%)
  between operations  16.3 us (9%)
  other arithmetic  8.81 us (5%)
    psum x1, waiting for transfers between devices, local(): grad_piece = lax.psum(grad_piece, 'space').astype(jnp.float32)  32.7 us
    ppermute x7, waiting for transfers between devices, local(): lax.ppermute(ring[-1], 'dp', [(dev, (dev + 1) % 8) for dev in range(8)])  31.4 us
    dot_general x9, matrix products, local(): lax.dot_general(cot_window, tap_weights[tap_index], (((1,), (1,)), ((), (...  14.4 us
    dot_general x9, matrix products, local(): jnp.dot(window, tap_weights[row_off * 3 + col_off], preferred_element_typ...  12.6 us
    ppermute x8, starting transfers between devices, space_sum(): lax.ppermute(parts, axis, pairs)  11.6 us
    ppermute x8, waiting for transfers between devices, space_sum(): lax.ppermute(parts, axis, pairs)  9.65 us
    concatenate x1, local copies, waits for them, and re-layouts, local(): jnp.roll(jnp.concatenate(ring[::-1], axis=0), (lax.axis_index('dp') + 1)...  7.64 us
    slice x9, local copies, waits for them, and re-layouts, local(): cot_pad[2 - row_off:2 - row_off + height_dev, 2 - col_off:2 - col_off + w...  7.52 us
  transfers between devices with their start and end apart: 21, of which 13 were waited for; matrix products, arithmetic and copies ran while one was open for 35% of the time, Pallas kernels for 0%

profile of v1, /device:TPU:0, one launch (start us, length us, event | category | flops | bytes accessed | tf_op | source)
XLA Modules:
  0.0 178.9 jit_solution(14504432050021784574)
XLA Ops:
  8.7 1.1 multiply_reduce_fusion.1
  10.1 3.1 %collective-permute-start = (f32[32]{0:T(128)S(1)}, f32[32]{0:T(128)S(1)}, u32[]{:S(2)}, u32[]{:S(2)}) collective-permute-start(f32[32]{0:T(128)S(1)} %reduce_sum.51), channel_id=1, source_target_pairs={{0,8},{8,0},{16,24},{24,16},{1,9},{9,1},{17,25},{25,17},{2,10},{10... | collective-permute-start | bytes 392 | tf_op jit(solution)/shard_map/ppermute | solution.py:33
  13.5 1.0 bitcast_multiply_fusion.2
  14.5 3.9 %collective-permute-start.13 = (bf16[1,128,320]{1,2,0:T(8,128)(2,1)S(1)}, bf16[1,128,320]{1,2,0:T(8,128)(2,1)S(1)}, u32[]{:S(2)}, u32[]{:S(2)}) collective-permute-start(bf16[1,128,320]{1,2,0:T(8,128)(2,1)S(1)} %get-tuple-element.26), channel_id=1, source_target_pairs={{0,8},{8,16},{16,24},{1,9},{9,17},{17,25},{2,10},{10,18},{18,26},{... | collective-permute-start | bytes 245768 | tf_op jit(solution)/shard_map/ppermute | solution.py:17
  18.4 1.3 collective-permute-start.14
  19.7 0.7 fusion.123
  20.4 1.1 copy.21
  21.5 1.2 copy.33
  22.7 0.8 bitcast_multiply_fusion.1
  23.5 3.7 %collective-permute-start.1 = (f32[32]{0:T(128)S(1)}, f32[32]{0:T(128)S(1)}, u32[]{:S(2)}, u32[]{:S(2)}) collective-permute-start(f32[32]{0:T(128)S(1)} %add.176), channel_id=1, source_target_pairs={{0,16},{8,24},{16,0},{24,8},{1,17},{9,25},{17,1},{25,9},{2,18},{10... | collective-permute-start | bytes 392 | tf_op jit(solution)/shard_map/ppermute | solution.py:33
  27.5 1.2 collective-permute-done.1
  28.7 2.9 %collective-permute-done.3 = f32[32]{0:T(128)S(1)} collective-permute-done((f32[32]{0:T(128)S(1)}, f32[32]{0:T(128)S(1)}, u32[]{:S(2)}, u32[]{:S(2)}) %collective-permute-start.3) | collective-permute-done | bytes 160 | tf_op jit(solution)/shard_map/ppermute | solution.py:33
  32.4 3.5 %collective-permute-start.4 = (bf16[1,128,320]{1,2,0:T(8,128)(2,1)S(1)}, bf16[1,128,320]{1,2,0:T(8,128)(2,1)S(1)}, u32[]{:S(2)}, u32[]{:S(2)}) collective-permute-start(bf16[1,128,320]{1,2,0:T(8,128)(2,1)S(1)} %get-tuple-element.30), channel_id=1, source_target_pairs={{0,8},{8,16},{16,24},{1,9},{9,17},{17,25},{2,10},{10,18},{18,26},{... | collective-permute-start | bytes 245768 | tf_op jit(solution)/shard_map/ppermute | solution.py:17
  35.9 1.3 collective-permute-start.5
  37.9 0.9 copy.32
  38.8 0.9 copy.31
  39.7 0.9 copy.34
  40.6 0.9 copy.35
  41.5 0.9 copy.37
  42.4 0.9 copy.30
  43.3 0.9 copy.36
  44.2 0.9 copy.29
  45.2 0.7 copy-done.24
  46.6 1.4 fusion.138
  49.1 6.4 %collective-permute-done.7 = bf16[360,320]{0,1:T(8,128)(2,1)S(1)} collective-permute-done((bf16[360,320]{0,1:T(8,128)(2,1)}, bf16[360,320]{0,1:T(8,128)(2,1)S(1)}, u32[]{:S(2)}, u32[]{:S(2)}) %collective-permute-start.7) | collective-permute-done | bytes 230432 | tf_op jit(solution)/shard_map/ppermute | solution.py:64
  55.5 0.5 fusion.35
  56.0 6.0 %collective-permute-done.8 = bf16[360,320]{0,1:T(8,128)(2,1)S(1)} collective-permute-done((bf16[360,320]{0,1:T(8,128)(2,1)S(1)}, bf16[360,320]{0,1:T(8,128)(2,1)S(1)}, u32[]{:S(2)}, u32[]{:S(2)}) %collective-permute-start.8) | collective-permute-done | bytes 230432 | tf_op jit(solution)/shard_map/ppermute | solution.py:64
  62.4 6.1 %collective-permute-done.9 = bf16[360,320]{0,1:T(8,128)(2,1)S(1)} collective-permute-done((bf16[360,320]{0,1:T(8,128)(2,1)S(1)}, bf16[360,320]{0,1:T(8,128)(2,1)S(1)}, u32[]{:S(2)}, u32[]{:S(2)}) %collective-permute-start.9) | collective-permute-done | bytes 230432 | tf_op jit(solution)/shard_map/ppermute | solution.py:64
  68.9 6.2 %collective-permute-done.10 = bf16[360,320]{0,1:T(8,128)(2,1)S(1)} collective-permute-done((bf16[360,320]{0,1:T(8,128)(2,1)S(1)}, bf16[360,320]{0,1:T(8,128)(2,1)S(1)}, u32[]{:S(2)}, u32[]{:S(2)}) %collective-permute-start.10) | collective-permute-done | bytes 230432 | tf_op jit(solution)/shard_map/ppermute | solution.py:64
  75.4 6.3 %collective-permute-done.11 = bf16[360,320]{0,1:T(8,128)(2,1)} collective-permute-done((bf16[360,320]{0,1:T(8,128)(2,1)S(1)}, bf16[360,320]{0,1:T(8,128)(2,1)}, u32[]{:S(2)}, u32[]{:S(2)}) %collective-permute-start.11) | collective-permute-done | bytes 230432 | tf_op jit(solution)/shard_map/ppermute | solution.py:64
  81.7 0.4 fusion.29
  82.1 2.6 %copy.41 = bf16[8,360,320]{1,2,0:T(8,128)(2,1)} copy(bf16[8,360,320]{2,1,0:T(8,128)(2,1)S(1)} %bitcast.202) | data formatting | bytes 3686400 | tf_op jit(solution)/shard_map/convert_element_type | solution.py:123
  85.0 1.3 copy.26
  88.0 0.5 collective-permute-done.12
  88.5 7.6 %concatenate.25 = bf16[5760,320]{0,1:T(8,128)(2,1)} concatenate(bf16[360,320]{0,1:T(8,128)(2,1)} %collective-permute-done.12, bf16[360,320]{0,1:T(8,128)(2,1)} %collective-permute-done.11, bf16[360,320]{0,1:T(8,128)(2,1)} %copy-done.19, bf16[360,320]{0,1:T(8,128)(2,1)} %copy-done.18, bf16[360,320]{0,1:T(8,128)(2,1)} %copy-done.17, bf16[360,320]{0,1:T(8,128)(2,1)} %copy-done.16, ...), dimensions={0} | concatenate | bytes 7372800 | tf_op jit(solution)/shard_map/jit(_roll_dynamic)/concatenate | solution.py:65
  96.2 1.4 fusion.72
  97.6 1.4 fusion.80
  98.9 1.4 fusion.84
  100.3 1.4 fusion.91
  101.7 1.4 fusion.95
  103.0 1.4 fusion.76
  104.4 1.4 fusion.99
  105.8 1.6 fusion.69
  107.4 1.4 fusion.14
  109.3 0.5 copy-done.7
  109.8 1.5 fusion.89
  111.3 1.6 fusion.93
  112.9 1.6 fusion.82
  114.5 1.6 fusion.78
  116.1 1.6 fusion.70
  117.7 1.5 fusion.97
  119.2 1.6 fusion.74
  120.8 1.5 fusion.86
  122.4 2.0 %fusion.136 = (f32[320]{0:T(512)S(1)}, f32[320]{0:T(512)S(1)}, f32[384,320]{0,1:T(8,128)S(1)}) fusion(f32[320]{0:T(512)S(1)} %mul.299, f32[320]{0:T(512)S(1)} %sub.59, f32[384,320]{0,1:T(8,128)S(1)} %copy.22, f32[384]{0:T(512)S(1)} %copy-done.30, f32[320]{0:T(512)S(1)} %copy-done.27, f32[320]{0:T(512)S(1)} %copy-done.29, f32[384,320]{0,1:T(8,128)S(1)} %fusion.70, ...), kind=kOutput, calls=%fused_computation.183 | convolution fusion | flops 81960320 | bytes 5415940 | tf_op jit(solution)/shard_map/dot_general | solution.py:109
  124.6 2.6 %collective-permute-start.15 = (f32[32]{0:T(128)S(1)}, f32[32]{0:T(128)S(1)}, u32[]{:S(2)}, u32[]{:S(2)}) collective-permute-start(f32[32]{0:T(128)S(1)} %reduce_sum.72), channel_id=1, source_target_pairs={{0,8},{8,0},{16,24},{24,16},{1,9},{9,1},{17,25},{25,17},{2,10},{10... | collective-permute-start | bytes 392 | tf_op jit(solution)/shard_map/ppermute | solution.py:33
  127.7 1.0 collective-permute-done.15
  128.7 1.4 collective-permute-start.16
  130.1 0.9 collective-permute-done.17
  131.0 0.6 collective-permute-start.18
  131.9 1.3 collective-permute-done.16
  133.2 2.3 %collective-permute-done.18 = f32[32]{0:T(128)S(1)} collective-permute-done((f32[32]{0:T(128)S(1)}, f32[32]{0:T(128)S(1)}, u32[]{:S(2)}, u32[]{:S(2)}) %collective-permute-start.18) | collective-permute-done | bytes 160 | tf_op jit(solution)/shard_map/ppermute | solution.py:33
  135.9 1.3 multiply_convert_fusion.1
  137.2 32.7 %all-reduce.4.cloned.1.call-done = bf16[360,320]{0,1:T(8,128)(2,1)} async-done(((bf16[360,320]{0,1:T(8,128)(2,1)}), bf16[360,320]{0,1:T(8,128)(2,1)}) %all-reduce.4.cloned.1.call-update) | async-done | bytes 230416 | tf_op jit(solution)/shard_map/psum | solution.py:129
  169.8 2.2 %fusion.47 = (f32[360,320]{0,1:T(8,128)}, f32[360,320]{0,1:T(8,128)}) fusion(f32[360,320]{0,1:T(8,128)S(1)} %copy-done.20, f32[360,320]{0,1:T(8,128)S(1)} %copy-done.21, bf16[360,320]{0,1:T(8,128)(2,1)} %all-reduce.4.cloned.1.call-done), kind=kLoop, calls=%fused_computation.65 | loop fusion | flops 1382400 | bytes 2073600 | tf_op jit(solution)/shard_map/div | solution.py:139
  (140 shorter events, 9.1 us)
Async XLA Ops:
  7.2 24.8 %copy-start = (bf16[1,3,128,320]{2,3,1,0:T(8,128)(2,1)S(1)}, bf16[1,3,128,320]{2,3,1,0:T(8,128)(2,1)}, u32[]{:S(2)}) copy-start(bf16[1,3,128,320]{2,3,1,0:T(8,128)(2,1)} %param.9) | copy-start | bytes 737284
  7.2 24.8 %copy-start.28 = (f32[320]{0:T(512)S(1)}, f32[320]{0:T(512)}, u32[]{:S(2)}) copy-start(f32[320]{0:T(512)} %param.11) | copy-start | bytes 3844
  7.2 24.8 %copy-start.27 = (f32[320]{0:T(512)S(1)}, f32[320]{0:T(512)}, u32[]{:S(2)}) copy-start(f32[320]{0:T(512)} %param.12) | copy-start | bytes 3844
  7.2 128.7 %reduce-scatter.2.cloned.1.call-start = ((), (), s32[]{:S(2)}) async-start(), calls=%async_computation.1 | async-start | bytes 2211840 | tf_op jit(solution)/shard_map/reduce_scatter | solution.py:122
  8.7 22.9 %copy-start.31 = (bf16[3,128]{1,0:T(4,128)(2,1)}, bf16[3,128]{1,0:T(4,128)(2,1)S(1)}, u32[]{:S(2)}) copy-start(bf16[3,128]{1,0:T(4,128)(2,1)S(1)} %get-tuple-element.37) | copy-start | bytes 2308
  10.1 13.4 %collective-permute-start = (f32[32]{0:T(128)S(1)}, f32[32]{0:T(128)S(1)}, u32[]{:S(2)}, u32[]{:S(2)}) collective-permute-start(f32[32]{0:T(128)S(1)} %reduce_sum.51), channel_id=1, source_target_pairs={{0,8},{8,0},{16,24},{24,16},{1,9},{9,1},{17,25},{25,17},{2,10},{10... | collective-permute-start | bytes 392 | tf_op jit(solution)/shard_map/ppermute | solution.py:33
  13.4 13.8 %collective-permute-start.2 = (f32[32]{0:T(128)S(1)}, f32[32]{0:T(128)S(1)}, u32[]{:S(2)}, u32[]{:S(2)}) collective-permute-start(f32[32]{0:T(128)S(1)} %reduce_sum.54), channel_id=1, source_target_pairs={{0,8},{8,0},{16,24},{24,16},{1,9},{9,1},{17,25},{25,17},{2,10},{10... | collective-permute-start | bytes 392 | tf_op jit(solution)/shard_map/ppermute | solution.py:33
  13.5 35.2 %collective-permute-start.6 = (bf16[360,320]{0,1:T(8,128)(2,1)}, bf16[360,320]{0,1:T(8,128)(2,1)}, u32[]{:S(2)}, u32[]{:S(2)}) collective-permute-start(bf16[360,320]{0,1:T(8,128)(2,1)} %param.13), channel_id=1, source_target_pairs={{0,1},{1,2},{2,3},{3,4},{4,5},{5,6},{6,7},{7,0},{8,9},{9,10},{10,1... | collective-permute-start | bytes 691208 | tf_op jit(solution)/shard_map/ppermute | solution.py:64
  14.5 22.6 %collective-permute-start.13 = (bf16[1,128,320]{1,2,0:T(8,128)(2,1)S(1)}, bf16[1,128,320]{1,2,0:T(8,128)(2,1)S(1)}, u32[]{:S(2)}, u32[]{:S(2)}) collective-permute-start(bf16[1,128,320]{1,2,0:T(8,128)(2,1)S(1)} %get-tuple-element.26), channel_id=1, source_target_pairs={{0,8},{8,16},{16,24},{1,9},{9,17},{17,25},{2,10},{10,18},{18,26},{... | collective-permute-start | bytes 245768 | tf_op jit(solution)/shard_map/ppermute | solution.py:17
  18.4 18.8 %collective-permute-start.14 = (bf16[1,128,320]{1,2,0:T(8,128)(2,1)S(1)}, bf16[1,128,320]{1,2,0:T(8,128)(2,1)S(1)}, u32[]{:S(2)}, u32[]{:S(2)}) collective-permute-start(bf16[1,128,320]{1,2,0:T(8,128)(2,1)S(1)} %get-tuple-element.27), channel_id=1, source_target_pairs={{8,0},{16,8},{24,16},{9,1},{17,9},{25,17},{10,2},{18,10},{26,18},{... | collective-permute-start | bytes 245768 | tf_op jit(solution)/shard_map/ppermute | solution.py:19
  23.5 5.2 %collective-permute-start.1 = (f32[32]{0:T(128)S(1)}, f32[32]{0:T(128)S(1)}, u32[]{:S(2)}, u32[]{:S(2)}) collective-permute-start(f32[32]{0:T(128)S(1)} %add.176), channel_id=1, source_target_pairs={{0,16},{8,24},{16,0},{24,8},{1,17},{9,25},{17,1},{25,9},{2,18},{10... | collective-permute-start | bytes 392 | tf_op jit(solution)/shard_map/ppermute | solution.py:33
  27.2 4.4 %collective-permute-start.3 = (f32[32]{0:T(128)S(1)}, f32[32]{0:T(128)S(1)}, u32[]{:S(2)}, u32[]{:S(2)}) collective-permute-start(f32[32]{0:T(128)S(1)} %add.178), channel_id=1, source_target_pairs={{0,16},{8,24},{16,0},{24,8},{1,17},{9,25},{17,1},{25,9},{2,18},{10... | collective-permute-start | bytes 392 | tf_op jit(solution)/shard_map/ppermute | solution.py:33
  32.4 12.8 %collective-permute-start.4 = (bf16[1,128,320]{1,2,0:T(8,128)(2,1)S(1)}, bf16[1,128,320]{1,2,0:T(8,128)(2,1)S(1)}, u32[]{:S(2)}, u32[]{:S(2)}) collective-permute-start(bf16[1,128,320]{1,2,0:T(8,128)(2,1)S(1)} %get-tuple-element.30), channel_id=1, source_target_pairs={{0,8},{8,16},{16,24},{1,9},{9,17},{17,25},{2,10},{10,18},{18,26},{... | collective-permute-start | bytes 245768 | tf_op jit(solution)/shard_map/ppermute | solution.py:17
  35.9 9.3 %collective-permute-start.5 = (bf16[1,128,320]{1,2,0:T(8,128)(2,1)S(1)}, bf16[1,128,320]{1,2,0:T(8,128)(2,1)S(1)}, u32[]{:S(2)}, u32[]{:S(2)}) collective-permute-start(bf16[1,128,320]{1,2,0:T(8,128)(2,1)S(1)} %get-tuple-element.31), channel_id=1, source_target_pairs={{8,0},{16,8},{24,16},{9,1},{17,9},{25,17},{10,2},{18,10},{26,18},{... | collective-permute-start | bytes 245768 | tf_op jit(solution)/shard_map/ppermute | solution.py:19
  45.1 2.8 %copy-start.22 = (bf16[1,128,320]{1,2,0:T(8,128)(2,1)}, bf16[1,128,320]{1,2,0:T(8,128)(2,1)S(1)}, u32[]{:S(2)}) copy-start(bf16[1,128,320]{1,2,0:T(8,128)(2,1)S(1)} %collective-permute-done.4) | copy-start | bytes 245764
  45.2 0.7 copy-start.24
  46.5 9.0 %copy-start.10 = (bf16[1,3,128,320]{2,3,1,0:T(8,128)(2,1)S(1)}, bf16[1,3,128,320]{2,3,1,0:T(8,128)(2,1)}, u32[]{:S(2)}) copy-start(bf16[1,3,128,320]{2,3,1,0:T(8,128)(2,1)} %param.10) | copy-start | bytes 737284
  46.5 9.0 %copy-start.32 = (bf16[3,128]{1,0:T(4,128)(2,1)S(1)}, bf16[3,128]{1,0:T(4,128)(2,1)}, u32[]{:S(2)}) copy-start(bf16[3,128]{1,0:T(4,128)(2,1)} %copy-done.31) | copy-start | bytes 2308
  48.7 6.8 %collective-permute-start.7 = (bf16[360,320]{0,1:T(8,128)(2,1)}, bf16[360,320]{0,1:T(8,128)(2,1)S(1)}, u32[]{:S(2)}, u32[]{:S(2)}) collective-permute-start(bf16[360,320]{0,1:T(8,128)(2,1)} %collective-permute-done.6), channel_id=1, source_target_pairs={{0,1},{1,2},{2,3},{3,4},{4,5},{5,6},{6,7},{7,0},{8,9},{9,10},{10,1... | collective-permute-start | bytes 691208 | tf_op jit(solution)/shard_map/ppermute | solution.py:64
  49.1 26.0 %copy-start.25 = (bf16[1,128,320]{1,2,0:T(8,128)(2,1)S(1)}, bf16[1,128,320]{1,2,0:T(8,128)(2,1)}, u32[]{:S(2)}) copy-start(bf16[1,128,320]{1,2,0:T(8,128)(2,1)} %copy-done.24) | copy-start | bytes 245764
  55.5 6.9 %copy-start.16 = (bf16[360,320]{0,1:T(8,128)(2,1)}, bf16[360,320]{0,1:T(8,128)(2,1)S(1)}, u32[]{:S(2)}) copy-start(bf16[360,320]{0,1:T(8,128)(2,1)S(1)} %collective-permute-done.7) | copy-start | bytes 691204
  55.5 6.5 %collective-permute-start.8 = (bf16[360,320]{0,1:T(8,128)(2,1)S(1)}, bf16[360,320]{0,1:T(8,128)(2,1)S(1)}, u32[]{:S(2)}, u32[]{:S(2)}) collective-permute-start(bf16[360,320]{0,1:T(8,128)(2,1)S(1)} %collective-permute-done.7), channel_id=1, source_target_pairs={{0,1},{1,2},{2,3},{3,4},{4,5},{5,6},{6,7},{7,0},{8,9},{9,10},{10,1... | collective-permute-start | bytes 691208 | tf_op jit(solution)/shard_map/ppermute | solution.py:64
  62.0 20.1 %copy-start.17 = (bf16[360,320]{0,1:T(8,128)(2,1)}, bf16[360,320]{0,1:T(8,128)(2,1)S(1)}, u32[]{:S(2)}) copy-start(bf16[360,320]{0,1:T(8,128)(2,1)S(1)} %collective-permute-done.8) | copy-start | bytes 691204
  62.0 6.5 %collective-permute-start.9 = (bf16[360,320]{0,1:T(8,128)(2,1)S(1)}, bf16[360,320]{0,1:T(8,128)(2,1)S(1)}, u32[]{:S(2)}, u32[]{:S(2)}) collective-permute-start(bf16[360,320]{0,1:T(8,128)(2,1)S(1)} %collective-permute-done.8), channel_id=1, source_target_pairs={{0,1},{1,2},{2,3},{3,4},{4,5},{5,6},{6,7},{7,0},{8,9},{9,10},{10,1... | collective-permute-start | bytes 691208 | tf_op jit(solution)/shard_map/ppermute | solution.py:64
  68.5 13.6 %copy-start.18 = (bf16[360,320]{0,1:T(8,128)(2,1)}, bf16[360,320]{0,1:T(8,128)(2,1)S(1)}, u32[]{:S(2)}) copy-start(bf16[360,320]{0,1:T(8,128)(2,1)S(1)} %collective-permute-done.9) | copy-start | bytes 691204
  68.5 6.5 %collective-permute-start.10 = (bf16[360,320]{0,1:T(8,128)(2,1)S(1)}, bf16[360,320]{0,1:T(8,128)(2,1)S(1)}, u32[]{:S(2)}, u32[]{:S(2)}) collective-permute-start(bf16[360,320]{0,1:T(8,128)(2,1)S(1)} %collective-permute-done.9), channel_id=1, source_target_pairs={{0,1},{1,2},{2,3},{3,4},{4,5},{5,6},{6,7},{7,0},{8,9},{9,10},{10,1... | collective-permute-start | bytes 691208 | tf_op jit(solution)/shard_map/ppermute | solution.py:64
  75.1 7.0 %copy-start.19 = (bf16[360,320]{0,1:T(8,128)(2,1)}, bf16[360,320]{0,1:T(8,128)(2,1)S(1)}, u32[]{:S(2)}) copy-start(bf16[360,320]{0,1:T(8,128)(2,1)S(1)} %collective-permute-done.10) | copy-start | bytes 691204
  75.1 6.6 %collective-permute-start.11 = (bf16[360,320]{0,1:T(8,128)(2,1)S(1)}, bf16[360,320]{0,1:T(8,128)(2,1)}, u32[]{:S(2)}, u32[]{:S(2)}) collective-permute-start(bf16[360,320]{0,1:T(8,128)(2,1)S(1)} %collective-permute-done.10), channel_id=1, source_target_pairs={{0,1},{1,2},{2,3},{3,4},{4,5},{5,6},{6,7},{7,0},{8,9},{9,10},{10,1... | collective-permute-start | bytes 691208 | tf_op jit(solution)/shard_map/ppermute | solution.py:64
  81.7 6.8 %collective-permute-start.12 = (bf16[360,320]{0,1:T(8,128)(2,1)}, bf16[360,320]{0,1:T(8,128)(2,1)}, u32[]{:S(2)}, u32[]{:S(2)}) collective-permute-start(bf16[360,320]{0,1:T(8,128)(2,1)} %collective-permute-done.11), channel_id=1, source_target_pairs={{0,1},{1,2},{2,3},{3,4},{4,5},{5,6},{6,7},{7,0},{8,9},{9,10},{10,1... | collective-permute-start | bytes 691208 | tf_op jit(solution)/shard_map/ppermute | solution.py:64
  84.7 1.6 copy-start.15
  84.7 1.9 %copy-start.14 = (bf16[3,128,320]{1,2,0:T(8,128)(2,1)S(1)}, bf16[3,128,320]{1,2,0:T(8,128)(2,1)}, u32[]{:S(2)}) copy-start(bf16[3,128,320]{1,2,0:T(8,128)(2,1)} %get-tuple-element.20) | copy-start | bytes 737284
  84.7 2.1 %copy-start.13 = (bf16[3,128,320]{1,2,0:T(8,128)(2,1)S(1)}, bf16[3,128,320]{1,2,0:T(8,128)(2,1)}, u32[]{:S(2)}) copy-start(bf16[3,128,320]{1,2,0:T(8,128)(2,1)} %get-tuple-element.21) | copy-start | bytes 737284
  84.7 2.3 %copy-start.12 = (bf16[3,128,320]{1,2,0:T(8,128)(2,1)S(1)}, bf16[3,128,320]{1,2,0:T(8,128)(2,1)}, u32[]{:S(2)}) copy-start(bf16[3,128,320]{1,2,0:T(8,128)(2,1)} %get-tuple-element.22) | copy-start | bytes 737284
  84.7 2.6 %copy-start.23 = (bf16[1,128,320]{1,2,0:T(8,128)(2,1)S(1)}, bf16[1,128,320]{1,2,0:T(8,128)(2,1)}, u32[]{:S(2)}) copy-start(bf16[1,128,320]{1,2,0:T(8,128)(2,1)} %copy-done.22) | copy-start | bytes 245764
  84.7 2.6 %copy-start.26 = (bf16[1,128,320]{1,2,0:T(8,128)(2,1)S(1)}, bf16[1,128,320]{1,2,0:T(8,128)(2,1)}, u32[]{:S(2)}) copy-start(bf16[1,128,320]{1,2,0:T(8,128)(2,1)} %copy-done.24) | copy-start | bytes 245764
  84.8 85.1 %all-reduce.4.cloned.1.call-start = ((), (), s32[]{:S(2)}) async-start(), calls=%async_computation.2 | async-start | bytes 491520 | tf_op jit(solution)/shard_map/psum | solution.py:129
  86.3 1.4 copy-start.11
  100.3 5.5 %copy-start.29 = (f32[320]{0:T(512)S(1)}, f32[320]{0:T(512)}, u32[]{:S(2)}) copy-start(f32[320]{0:T(512)} %param.11) | copy-start | bytes 3844
  100.3 5.5 %copy-start.33 = (f32[384]{0:T(512)S(1)}, f32[384]{0:T(512)}, u32[]{:S(2)}) copy-start(f32[384]{0:T(512)} %get-tuple-element.36) | copy-start | bytes 4612
  108.9 1.0 copy-start.7
  108.9 2.5 %copy-start.6 = (bf16[3,128,320]{2,1,0:T(8,128)(2,1)S(1)}, bf16[3,128,320]{2,1,0:T(8,128)(2,1)}, u32[]{:S(2)}) copy-start(bf16[3,128,320]{2,1,0:T(8,128)(2,1)} %copy.31) | copy-start | bytes 737284
  108.9 4.1 %copy-start.5 = (bf16[3,128,320]{2,1,0:T(8,128)(2,1)S(1)}, bf16[3,128,320]{2,1,0:T(8,128)(2,1)}, u32[]{:S(2)}) copy-start(bf16[3,128,320]{2,1,0:T(8,128)(2,1)} %copy.34) | copy-start | bytes 737284
  109.1 5.4 %copy-start.4 = (bf16[3,128,320]{2,1,0:T(8,128)(2,1)S(1)}, bf16[3,128,320]{2,1,0:T(8,128)(2,1)}, u32[]{:S(2)}) copy-start(bf16[3,128,320]{2,1,0:T(8,128)(2,1)} %copy.35) | copy-start | bytes 737284
  109.3 6.8 %copy-start.3 = (bf16[3,128,320]{2,1,0:T(8,128)(2,1)S(1)}, bf16[3,128,320]{2,1,0:T(8,128)(2,1)}, u32[]{:S(2)}) copy-start(bf16[3,128,320]{2,1,0:T(8,128)(2,1)} %copy.37) | copy-start | bytes 737284
  111.3 6.4 %copy-start.8 = (bf16[3,128,320]{2,1,0:T(8,128)(2,1)S(1)}, bf16[3,128,320]{2,1,0:T(8,128)(2,1)}, u32[]{:S(2)}) copy-start(bf16[3,128,320]{2,1,0:T(8,128)(2,1)} %copy.30) | copy-start | bytes 737284
  112.9 6.3 %copy-start.9 = (bf16[3,128,320]{2,1,0:T(8,128)(2,1)S(1)}, bf16[3,128,320]{2,1,0:T(8,128)(2,1)}, u32[]{:S(2)}) copy-start(bf16[3,128,320]{2,1,0:T(8,128)(2,1)} %copy.36) | copy-start | bytes 737284
  114.5 6.3 %copy-start.2 = (bf16[384,320]{1,0:T(8,128)(2,1)S(1)}, bf16[384,320]{1,0:T(8,128)(2,1)}, u32[]{:S(2)}) copy-start(bf16[384,320]{1,0:T(8,128)(2,1)} %bitcast_multiply_fusion.1) | copy-start | bytes 737284
  116.1 6.2 %copy-start.1 = (bf16[3,128,320]{2,1,0:T(8,128)(2,1)S(1)}, bf16[3,128,320]{2,1,0:T(8,128)(2,1)}, u32[]{:S(2)}) copy-start(bf16[3,128,320]{2,1,0:T(8,128)(2,1)} %copy.29) | copy-start | bytes 737284
  116.1 6.2 %copy-start.30 = (f32[384]{0:T(512)S(1)}, f32[384]{0:T(512)}, u32[]{:S(2)}) copy-start(f32[384]{0:T(512)} %get-tuple-element.34) | copy-start | bytes 4612
  124.4 45.5 %copy-start.20 = (f32[360,320]{0,1:T(8,128)S(1)}, f32[360,320]{0,1:T(8,128)}, u32[]{:S(2)}) copy-start(f32[360,320]{0,1:T(8,128)} %param.15) | copy-start | bytes 1382404
  124.4 45.4 %copy-start.21 = (f32[360,320]{0,1:T(8,128)S(1)}, f32[360,320]{0,1:T(8,128)}, u32[]{:S(2)}) copy-start(f32[360,320]{0,1:T(8,128)} %param.14) | copy-start | bytes 1382404
  124.6 4.1 %collective-permute-start.15 = (f32[32]{0:T(128)S(1)}, f32[32]{0:T(128)S(1)}, u32[]{:S(2)}, u32[]{:S(2)}) collective-permute-start(f32[32]{0:T(128)S(1)} %reduce_sum.72), channel_id=1, source_target_pairs={{0,8},{8,0},{16,24},{24,16},{1,9},{9,1},{17,25},{25,17},{2,10},{10... | collective-permute-start | bytes 392 | tf_op jit(solution)/shard_map/ppermute | solution.py:33
  127.4 3.6 %collective-permute-start.17 = (f32[32]{0:T(128)S(1)}, f32[32]{0:T(128)S(1)}, u32[]{:S(2)}, u32[]{:S(2)}) collective-permute-start(f32[32]{0:T(128)S(1)} %reduce_sum.75), channel_id=1, source_target_pairs={{0,8},{8,0},{16,24},{24,16},{1,9},{9,1},{17,25},{25,17},{2,10},{10... | collective-permute-start | bytes 392 | tf_op jit(solution)/shard_map/ppermute | solution.py:33
  128.7 4.4 %collective-permute-start.16 = (f32[32]{0:T(128)S(1)}, f32[32]{0:T(128)S(1)}, u32[]{:S(2)}, u32[]{:S(2)}) collective-permute-start(f32[32]{0:T(128)S(1)} %add.214), channel_id=1, source_target_pairs={{0,16},{8,24},{16,0},{24,8},{1,17},{9,25},{17,1},{25,9},{2,18},{10... | collective-permute-start | bytes 392 | tf_op jit(solution)/shard_map/ppermute | solution.py:33
  131.0 4.4 %collective-permute-start.18 = (f32[32]{0:T(128)S(1)}, f32[32]{0:T(128)S(1)}, u32[]{:S(2)}, u32[]{:S(2)}) collective-permute-start(f32[32]{0:T(128)S(1)} %add.216), channel_id=1, source_target_pairs={{0,16},{8,24},{16,0},{24,8},{1,17},{9,25},{17,1},{25,9},{2,18},{10... | collective-permute-start | bytes 392 | tf_op jit(solution)/shard_map/ppermute | solution.py:33
Sparse Core Ops, SparseCore 0:
  84.9 40.9 reduce-scatter.1
  136.0 33.7 all-reduce.3
